TPU v7x, 32 devices: a whole 2x2x4 slice. The times are simulated.
32 devices in a mesh: row: 8 (over z, y), col: 4 (over x, core).
Axes of the slice: x: 2, y: 2, z: 4, core: 2. Of those that a mesh axis runs over, the one named last changes fastest.
Arguments:
- gram: float32 [16384, 16384], P('row', 'col'), may hold values from -1 to 17, as said below
Outputs:
- factored: float32 [16384, 16384], P('row', 'col')
Inputs may be any that keep to these rules, and one draw needn't show every extreme that they name: gram holds a symmetric positive definite matrix in the block-cyclic order of the steps.
All inputs are finite; a program needn't handle non-finite values.
Results may differ from a plain program's by a relative error of at most 0.0001.
Values sent between devices are 32-bit elements; how exact they have to be, the bound alone decides.
No kernel may reach another device: no remote copies, remote signals or barrier semaphores. Data moves between devices by JAX's collectives and lax.ppermute only.
A program may use at most 192 MiB of HBM per device.

v0:
```python
import jax
import jax.numpy as jnp
from jax import lax
from jax.sharding import PartitionSpec as P

NB = 512
STEPS = 2


def broadcast(value, axis, source):
    kept = jnp.where(lax.axis_index(axis) == source, value, 0).astype(value.dtype)
    return lax.psum(kept, axis)


def from_partner(block, axis, apart):
    count = lax.axis_size(axis)
    route = []
    for low in range(count):
        high = low | 1 << apart
        if high != low and high < count:
            route += [(low, high), (high, low)]
    return lax.ppermute(block, axis, route)


def global_index(count, block, grid, position):
    ladder = jnp.arange(count, dtype=jnp.int32)
    return (ladder // block * grid + position) * block + ladder % block


def times_transposed(left, right):
    return lax.dot_general(
        left,
        right,
        (((1,), (1,)), ((), ())),
        precision=lax.Precision.HIGHEST,
        preferred_element_type=jnp.float32,
    )


def local(gram):
    grid_rows = lax.axis_size("row")
    grid_cols = lax.axis_size("col")
    row_id = lax.axis_index("row")
    col_id = lax.axis_index("col")
    rblock = NB * grid_cols // grid_rows
    per_class = grid_rows // grid_cols
    local_rows = gram.shape[0]
    local_cols = gram.shape[1]
    blocks = local_rows // rblock
    grows = global_index(local_rows, rblock, grid_rows, row_id)
    gcols = global_index(local_cols, NB, grid_cols, col_id)
    member = row_id % per_class
    row_class = row_id // per_class
    identity = jnp.eye(NB, dtype=jnp.float32)

    def factor_panel(matrix, panel_index):
        owner_col = panel_index % grid_cols
        local_block = panel_index // grid_cols
        end_row = panel_index * NB + NB
        column = matrix[:, local_block * NB : (local_block + 1) * NB]
        square = column[local_block * rblock : (local_block + 1) * rblock]
        is_owner = col_id == owner_col
        in_class = row_class == owner_col
        select = (jnp.arange(per_class, dtype=jnp.int32) == member).astype(jnp.float32)
        weight = jnp.where(is_owner & in_class, 1.0, 0.0).astype(jnp.float32)
        placed = (select[:, None, None] * square[None]).reshape(NB, NB) * weight
        diagonal = lax.psum(placed, "row")
        diagonal = jnp.where(is_owner, diagonal, identity)
        low_factor = jnp.linalg.cholesky(diagonal)
        inverse = jax.scipy.linalg.solve_triangular(low_factor, identity, lower=True)
        solved = times_transposed(column, inverse)
        trailing = jnp.where((grows >= end_row)[:, None], solved, 0.0)
        rows_diag = lax.dynamic_slice_in_dim(low_factor, member * rblock, rblock, 0)
        previous = trailing[local_block * rblock : (local_block + 1) * rblock]
        patched = jnp.where(in_class, rows_diag, previous)
        factored = trailing.at[local_block * rblock : (local_block + 1) * rblock].set(patched)
        new_column = jnp.where(is_owner, factored, column)
        matrix = matrix.at[:, local_block * NB : (local_block + 1) * NB].set(new_column)
        return (matrix, trailing)

    matrix = gram
    for panel_index in range(STEPS):
        matrix, trailing = factor_panel(matrix, panel_index)
        spread_owner_col = panel_index % grid_cols
        spread_rows_all = broadcast(trailing, "col", spread_owner_col)
        pieces = spread_rows_all.reshape(grid_cols, blocks // grid_cols * rblock, NB)
        shift_bits = per_class.bit_length() - 1
        for bit_level in reversed(range(grid_cols.bit_length() - 1)):
            halfway = pieces.shape[0] // 2
            own_bit = row_class >> bit_level & 1
            wanted = col_id >> bit_level & 1
            upper = own_bit == 1
            retained = jnp.where(upper, pieces[halfway:], pieces[:halfway])
            outgoing = jnp.where(upper, pieces[:halfway], pieces[halfway:])
            received = from_partner(outgoing, "row", shift_bits + bit_level)
            pieces = jnp.where(own_bit == wanted, retained, received)
        gathered = lax.all_gather(pieces[0], "row", axis=0, tiled=True)
        spread_columns = gathered.reshape(grid_cols, per_class, blocks // grid_cols, rblock, NB)
        spread_columns = jnp.transpose(spread_columns, (0, 2, 1, 3, 4)).reshape(local_cols, NB)
        first_row = panel_index * NB
        apply_end_row = first_row + NB
        current = matrix
        updated = current - times_transposed(spread_rows_all, spread_columns)
        panel_rows = (grows >= first_row) & (grows < apply_end_row)
        beyond = gcols >= apply_end_row
        updated = jnp.where(panel_rows[:, None] & beyond[None, :], 0.0, updated)
        matrix = matrix.at[:, 0:local_cols].set(updated)
    matrix, trailing = factor_panel(matrix, STEPS)
    return matrix


def solution(mesh):
    placed = (P("row", "col"),)
    return jax.shard_map(
        local, mesh=mesh, in_specs=placed, out_specs=P("row", "col"), check_vma=False
    )
```

profile of v0, /device:TPU:0, one launch (start us, length us, event | category | flops | bytes accessed | tf_op | source)
XLA Modules:
  0.0 1543.9 jit_solution(489001765417519902)
XLA Ops:
  6.5 23.0 %copy.106 = f32[2048,4096]{1,0:T(8,128)} copy(f32[2048,4096]{1,0:T(8,128)} %param.24) | data formatting | bytes 67108864
  32.8 81.1 %all-reduce.7.cloned.1.call-done = f32[512,512]{0,1:T(8,128)} async-done(((f32[512,512]{0,1:T(8,128)}), f32[512,512]{0,1:T(8,128)}) %all-reduce.7.cloned.1.call-update) | async-done | bytes 1048592 | tf_op jit(solution)/shard_map/psum | solution.py:67
  118.1 11.7 cholesky.374
  130.0 9.8 custom-call.31
  140.5 11.7 cholesky.393
  152.3 10.0 custom-call.32
  162.9 11.7 cholesky.414
  174.6 9.8 custom-call.33
  185.1 11.7 cholesky.431
  203.0 8.4 while.16
  211.4 39.3 %custom-call.34 = f32[4,128,128]{1,2,0:T(8,128)S(1)} custom-call(f32[4,128,128]{2,1,0:T(8,128)S(1)} %get-tuple-element.139), custom_call_target="InvertDiagBlocksLowerTriangular" | custom-call | tf_op jit(solution)/shard_map/jit(_solve_triangular)/triangular_solve | solution.py:70
  255.5 10.6 broadcast_select_fusion.1
  266.2 84.3 %all-reduce.9.cloned.1.call-done = f32[2048,512]{1,0:T(8,128)} async-done(((f32[2048,512]{1,0:T(8,128)}), f32[2048,512]{1,0:T(8,128)}) %all-reduce.9.cloned.1.call-update) | async-done | bytes 4194320 | tf_op jit(solution)/shard_map/psum | solution.py:12
  350.5 4.8 slice_select_fusion.2
  357.7 90.7 %collective-permute-done = f32[2,512,512]{2,1,0:T(8,128)S(1)} collective-permute-done((f32[2,512,512]{2,1,0:T(8,128)}, f32[2,512,512]{2,1,0:T(8,128)S(1)}, u32[]{:S(2)}, u32[]{:S(2)}) %collective-permute-start) | collective-permute-done | bytes 2097184 | tf_op jit(solution)/shard_map/ppermute | solution.py:22
  453.6 23.9 %collective-permute-done.1 = f32[1,512,512]{2,1,0:T(8,128)} collective-permute-done((f32[1,512,512]{2,1,0:T(8,128)}, f32[1,512,512]{2,1,0:T(8,128)}, u32[]{:S(2)}, u32[]{:S(2)}) %collective-permute-start.1) | collective-permute-done | bytes 1048608 | tf_op jit(solution)/shard_map/ppermute | solution.py:22
  482.2 7.1 fusion
  489.3 116.8 %all-gather.5.cloned.1.call-done = f32[1,4096,512]{2,1,0:T(8,128)} async-done(((f32[1,512,512]{2,1,0:T(8,128)}), f32[1,4096,512]{2,1,0:T(8,128)}) %all-gather.5.cloned.1.call-update) | async-done | bytes 8388624 | tf_op jit(solution)/shard_map/all_gather | solution.py:97
  610.7 60.7 %subtract_select_fusion.1 = f32[2048,4096]{1,0:T(8,128)} fusion(f32[2048,4096]{1,0:T(8,128)} %fusion, pred[4096]{0:T(1024)(128)(4,1)S(1)} %broadcast_compare_fusion.1, pred[2048]{0:T(1024)(128)(4,1)S(1)} %get-tuple-element.222, f32[2048,512]{1,0:T(8,128)S(1)} %copy-done, f32[4096,512]{1,0:T(8,128)S(1)} %bitcast.177), kind=kOutput, calls=%fused_computation.7 | convolution fusion | flops 51564773376 | bytes 79697920 | tf_op jit(solution)/shard_map/dot_general | solution.py:31
  674.6 76.4 %all-reduce.11.cloned.1.call-done = f32[512,512]{0,1:T(8,128)} async-done(((f32[512,512]{0,1:T(8,128)}), f32[512,512]{0,1:T(8,128)}) %all-reduce.11.cloned.1.call-update) | async-done | bytes 1048592 | tf_op jit(solution)/shard_map/psum | solution.py:67
  754.0 11.7 cholesky.446
  765.9 9.8 custom-call.35
  776.4 11.7 cholesky.465
  788.1 10.0 custom-call.36
  798.8 11.7 cholesky.486
  810.6 9.8 custom-call.37
  821.0 11.7 cholesky.503
  839.8 8.4 while.17
  848.2 39.3 %custom-call.38 = f32[4,128,128]{1,2,0:T(8,128)S(1)} custom-call(f32[4,128,128]{2,1,0:T(8,128)S(1)} %get-tuple-element.140), custom_call_target="InvertDiagBlocksLowerTriangular" | custom-call | tf_op jit(solution)/shard_map/jit(_solve_triangular)/triangular_solve | solution.py:70
  892.3 10.6 broadcast_select_fusion
  903.1 85.0 %all-reduce.13.cloned.1.call-done = f32[2048,512]{1,0:T(8,128)} async-done(((f32[2048,512]{1,0:T(8,128)}), f32[2048,512]{1,0:T(8,128)}) %all-reduce.13.cloned.1.call-update) | async-done | bytes 4194320 | tf_op jit(solution)/shard_map/psum | solution.py:12
  993.4 90.5 %collective-permute-done.2 = f32[2,512,512]{2,1,0:T(8,128)S(1)} collective-permute-done((f32[2,512,512]{2,1,0:T(8,128)S(1)}, f32[2,512,512]{2,1,0:T(8,128)S(1)}, u32[]{:S(2)}, u32[]{:S(2)}) %collective-permute-start.2) | collective-permute-done | bytes 2097184 | tf_op jit(solution)/shard_map/ppermute | solution.py:22
  1085.1 23.7 %collective-permute-done.3 = f32[1,512,512]{2,1,0:T(8,128)S(1)} collective-permute-done((f32[1,512,512]{2,1,0:T(8,128)S(1)}, f32[1,512,512]{2,1,0:T(8,128)S(1)}, u32[]{:S(2)}, u32[]{:S(2)}) %collective-permute-start.3) | collective-permute-done | bytes 1048608 | tf_op jit(solution)/shard_map/ppermute | solution.py:22
  1112.3 5.8 fusion.1
  1118.1 118.1 %all-gather.7.cloned.1.call-done = f32[1,4096,512]{2,1,0:T(8,128)} async-done(((f32[1,512,512]{2,1,0:T(8,128)}), f32[1,4096,512]{2,1,0:T(8,128)}) %all-gather.7.cloned.1.call-update) | async-done | bytes 8388624 | tf_op jit(solution)/shard_map/all_gather | solution.py:97
  1240.8 60.9 %subtract_select_fusion = f32[2048,4096]{1,0:T(8,128)} fusion(f32[2048,4096]{1,0:T(8,128)} %fusion.1, pred[4096]{0:T(1024)(128)(4,1)S(1)} %broadcast_compare_fusion, pred[2048]{0:T(1024)(128)(4,1)S(1)} %compare_and_fusion.1, f32[2048,512]{1,0:T(8,128)S(1)} %copy-done.1, f32[4096,512]{1,0:T(8,128)S(1)} %bitcast.178), kind=kOutput, calls=%fused_computation.6 | convolution fusion | flops 51564773376 | bytes 79697920 | tf_op jit(solution)/shard_map/dot_general | solution.py:31
  1304.6 76.6 %all-reduce.15.cloned.1.call-done = f32[512,512]{0,1:T(8,128)} async-done(((f32[512,512]{0,1:T(8,128)}), f32[512,512]{0,1:T(8,128)}) %all-reduce.15.cloned.1.call-update) | async-done | bytes 1048592 | tf_op jit(solution)/shard_map/psum | solution.py:67
  1384.3 11.7 cholesky.518
  1396.1 9.8 custom-call.39
  1406.6 11.7 cholesky.537
  1418.4 10.2 custom-call.40
  1429.3 11.7 cholesky.558
  1441.0 9.8 custom-call.41
  1451.4 11.9 cholesky.575
  1469.8 8.1 while.18
  1478.0 39.3 %custom-call.42 = f32[4,128,128]{1,2,0:T(8,128)S(1)} custom-call(f32[4,128,128]{2,1,0:T(8,128)S(1)} %get-tuple-element.141), custom_call_target="InvertDiagBlocksLowerTriangular" | custom-call | tf_op jit(solution)/shard_map/jit(_solve_triangular)/triangular_solve | solution.py:70
  1522.1 8.7 fusion.14
  1531.0 5.8 fusion.2
  (199 shorter events, 108.4 us)
Async XLA Ops:
  6.5 107.3 %all-reduce.7.cloned.1.call-start = ((), (), s32[]{:S(2)}) async-start(), calls=%async_computation | async-start | bytes 2097152 | tf_op jit(solution)/shard_map/psum | solution.py:67
  32.6 317.9 %all-reduce.9.cloned.1.call-start = ((), (), s32[]{:S(2)}) async-start(), calls=%async_computation.1 | async-start | bytes 8388608 | tf_op jit(solution)/shard_map/psum | solution.py:12
  113.9 2.8 copy-start.2
  266.2 340.0 %all-gather.5.cloned.1.call-start = ((), (), s32[]{:S(2)}) async-start(), calls=%async_computation.5 | async-start | bytes 9437184 | tf_op jit(solution)/shard_map/all_gather | solution.py:97
  355.3 93.1 %collective-permute-start = (f32[2,512,512]{2,1,0:T(8,128)}, f32[2,512,512]{2,1,0:T(8,128)S(1)}, u32[]{:S(2)}, u32[]{:S(2)}) collective-permute-start(f32[2,512,512]{2,1,0:T(8,128)} %bitcast.13), channel_id=1, source_target_pairs={{0,16},{16,0},{4,20},{20,4},{8,24},{24,8},{12,28},{28,12},{1,17},{... | collective-permute-start | bytes 6291464 | tf_op jit(solution)/shard_map/ppermute | solution.py:22
  448.4 1.3 copy-start.7
  453.0 24.5 %collective-permute-start.1 = (f32[1,512,512]{2,1,0:T(8,128)}, f32[1,512,512]{2,1,0:T(8,128)}, u32[]{:S(2)}, u32[]{:S(2)}) collective-permute-start(f32[1,512,512]{2,1,0:T(8,128)} %slice_select_fusion.5), channel_id=1, source_target_pairs={{0,8},{8,0},{4,12},{12,4},{16,24},{24,16},{20,28},{28,20},{1,9},{9... | collective-permute-start | bytes 3145736 | tf_op jit(solution)/shard_map/ppermute | solution.py:22
  478.9 272.1 %all-reduce.11.cloned.1.call-start = ((), (), s32[]{:S(2)}) async-start(), calls=%async_computation.2 | async-start | bytes 2097152 | tf_op jit(solution)/shard_map/psum | solution.py:67
  606.1 4.6 copy-start
  674.4 313.7 %all-reduce.13.cloned.1.call-start = ((), (), s32[]{:S(2)}) async-start(), calls=%async_computation.3 | async-start | bytes 8388608 | tf_op jit(solution)/shard_map/psum | solution.py:12
  751.0 1.5 copy-start.3
  902.9 333.3 %all-gather.7.cloned.1.call-start = ((), (), s32[]{:S(2)}) async-start(), calls=%async_computation.6 | async-start | bytes 9437184 | tf_op jit(solution)/shard_map/all_gather | solution.py:97
  990.9 93.0 %collective-permute-start.2 = (f32[2,512,512]{2,1,0:T(8,128)S(1)}, f32[2,512,512]{2,1,0:T(8,128)S(1)}, u32[]{:S(2)}, u32[]{:S(2)}) collective-permute-start(f32[2,512,512]{2,1,0:T(8,128)S(1)} %bitcast.189), channel_id=1, source_target_pairs={{0,16},{16,0},{4,20},{20,4},{8,24},{24,8},{12,28},{28,12},{1,17},{... | collective-permute-start | bytes 6291464 | tf_op jit(solution)/shard_map/ppermute | solution.py:22
  1084.3 26.0 %copy-start.5 = (f32[512,512]{1,0:T(8,128)S(1)}, f32[512,512]{1,0:T(8,128)}, u32[]{:S(2)}) copy-start(f32[512,512]{1,0:T(8,128)} %get-tuple-element.169) | copy-start | bytes 3145732
  1084.6 24.2 %collective-permute-start.3 = (f32[1,512,512]{2,1,0:T(8,128)S(1)}, f32[1,512,512]{2,1,0:T(8,128)S(1)}, u32[]{:S(2)}, u32[]{:S(2)}) collective-permute-start(f32[1,512,512]{2,1,0:T(8,128)S(1)} %slice_select_fusion.4), channel_id=1, source_target_pairs={{0,8},{8,0},{4,12},{12,4},{16,24},{24,16},{20,28},{28,20},{1,9},{9... | collective-permute-start | bytes 3145736 | tf_op jit(solution)/shard_map/ppermute | solution.py:22
  1110.2 271.1 %all-reduce.15.cloned.1.call-start = ((), (), s32[]{:S(2)}) async-start(), calls=%async_computation.4 | async-start | bytes 2097152 | tf_op jit(solution)/shard_map/psum | solution.py:67
  1236.2 4.6 copy-start.1
  1381.3 1.5 copy-start.4
  1522.1 8.7 copy-start.6
Sparse Core Ops, SparseCore 0:
  32.7 81.0 all-reduce.6
  266.3 84.1 all-reduce.8
  479.1 127.0 all-gather.4
  674.5 76.4 all-reduce.10
  903.0 85.0 all-reduce.12
  1110.3 125.8 all-gather.6
  1304.7 76.4 all-reduce.14
where the time goes:
time: 1550 us; the launch traced here: 1540 us
  waiting for transfers between devices  867 us (56%)
  other arithmetic  408 us (26%)
  matrix products  171 us (11%)
  local copies, waits for them, and re-layouts  67.9 us (4%)
  between operations  22.3 us (1%)
    another operation x44, other arithmetic, factor_panel(): low_factor = jnp.linalg.cholesky(diagonal)  238 us
    all_gather x2, waiting for transfers between devices, local(): gathered = lax.all_gather(pieces[0], 'row', axis=0, tiled=True)  235 us
    psum x3, waiting for transfers between devices, factor_panel(): diagonal = lax.psum(placed, 'row')  234 us
    ppermute x4, waiting for transfers between devices, from_partner(): return lax.ppermute(block, axis, route)  229 us
    psum x2, waiting for transfers between devices, broadcast(): return lax.psum(kept, axis)  169 us
    dot_general x5, matrix products, times_transposed(): lax.dot_general(left, right, (((1,), (1,)), ((), ())), precision=lax.Prec...  152 us
    another operation x7, other arithmetic, factor_panel(): jax.scipy.linalg.solve_triangular(low_factor, identity, lower=True)  122 us
  transfers between devices with their start and end apart: 11, of which 11 were waited for; matrix products, arithmetic and copies ran while one was open for 1% of the time, Pallas kernels for 0%

commit v1 on v0

--- a/solution.py
+++ b/solution.py
@@ -7,9 +7,15 @@
 STEPS = 2
 
 
+def record_fit(block_here, link_axis):
+    met_up = jax.lax.all_gather(block_here, link_axis)
+    then = jnp.sum(met_up, 0)
+    return then
+
+
 def broadcast(value, axis, source):
     kept = jnp.where(lax.axis_index(axis) == source, value, 0).astype(value.dtype)
-    return lax.psum(kept, axis)
+    return record_fit(kept, axis)
 
 
 def from_partner(block, axis, apart):

time: 1550 us -> 1630 us (1.052)
  waiting for transfers between devices: 867 us -> 909 us
  other arithmetic: 408 us -> 439 us
    all_gather x0 -> x2, waiting for transfers between devices: none -> 210 us  [record_fit(): met_up = jax.lax.all_gather(block_here, link_axis)]
    psum x2 -> x0, waiting for transfers between devices: 169 us -> none  [broadcast(): return lax.psum(kept, axis)]
    reduce_sum x0 -> x2, other arithmetic: none -> 20.6 us  [record_fit(): then = jnp.sum(met_up, 0)]
where the time goes in v1:
time: 1630 us; the launch traced here: 1620 us
  waiting for transfers between devices  909 us (56%)
  other arithmetic  439 us (27%)
  matrix products  171 us (10%)
  local copies, waits for them, and re-layouts  67.5 us (4%)
  between operations  22.3 us (1%)
    another operation x44, other arithmetic, factor_panel(): low_factor = jnp.linalg.cholesky(diagonal)  248 us
    psum x3, waiting for transfers between devices, factor_panel(): diagonal = lax.psum(placed, 'row')  234 us
    all_gather x2, waiting for transfers between devices, local(): gathered = lax.all_gather(pieces[0], 'row', axis=0, tiled=True)  233 us
    ppermute x4, waiting for transfers between devices, from_partner(): return lax.ppermute(block, axis, route)  231 us
    all_gather x2, waiting for transfers between devices, record_fit(): met_up = jax.lax.all_gather(block_here, link_axis)  210 us
    dot_general x5, matrix products, times_transposed(): lax.dot_general(left, right, (((1,), (1,)), ((), ())), precision=lax.Prec...  152 us
    another operation x7, other arithmetic, factor_panel(): jax.scipy.linalg.solve_triangular(low_factor, identity, lower=True)  122 us
  transfers between devices with their start and end apart: 11, of which 11 were waited for; matrix products, arithmetic and copies ran while one was open for 1% of the time, Pallas kernels for 0%

profile of v1, /device:TPU:0, one launch (start us, length us, event | category | flops | bytes accessed | tf_op | source)
XLA Modules:
  0.0 1615.8 jit_solution(1784925896366007515)
XLA Ops:
  6.5 23.0 %copy.106 = f32[2048,4096]{1,0:T(8,128)} copy(f32[2048,4096]{1,0:T(8,128)} %param.24) | data formatting | bytes 67108864
  32.8 81.1 %all-reduce.5.cloned.1.call-done = f32[512,512]{0,1:T(8,128)} async-done(((f32[512,512]{0,1:T(8,128)}), f32[512,512]{0,1:T(8,128)}) %all-reduce.5.cloned.1.call-update) | async-done | bytes 1048592 | tf_op jit(solution)/shard_map/psum | solution.py:73
  118.1 11.7 cholesky.374
  130.0 9.8 custom-call.31
  140.5 11.7 cholesky.393
  152.3 10.0 custom-call.32
  163.0 11.7 cholesky.414
  174.7 9.8 custom-call.33
  185.1 11.7 cholesky.431
  196.9 11.2 compare_reduce_fusion.9
  213.3 8.1 while.16
  221.5 39.3 %custom-call.34 = f32[4,128,128]{1,2,0:T(8,128)S(1)} custom-call(f32[4,128,128]{2,1,0:T(8,128)S(1)} %get-tuple-element.139), custom_call_target="InvertDiagBlocksLowerTriangular" | custom-call | tf_op jit(solution)/shard_map/jit(_solve_triangular)/triangular_solve | solution.py:76
  265.6 10.5 broadcast_select_fusion.1
  276.2 104.7 %all-gather.9.cloned.1.call-done = f32[8192,512]{1,0:T(8,128)} async-done(((f32[2048,512]{1,0:T(8,128)}), f32[8192,512]{1,0:T(8,128)}) %all-gather.9.cloned.1.call-update) | async-done | bytes 16777232 | tf_op jit(solution)/shard_map/all_gather | solution.py:11
  380.9 10.3 reduce_sum.18
  398.4 91.4 %collective-permute-done = f32[2,512,512]{2,1,0:T(8,128)S(1)} collective-permute-done((f32[2,512,512]{2,1,0:T(8,128)}, f32[2,512,512]{2,1,0:T(8,128)S(1)}, u32[]{:S(2)}, u32[]{:S(2)}) %collective-permute-start) | collective-permute-done | bytes 2097184 | tf_op jit(solution)/shard_map/ppermute | solution.py:28
  495.0 24.2 %collective-permute-done.1 = f32[1,512,512]{2,1,0:T(8,128)} collective-permute-done((f32[1,512,512]{2,1,0:T(8,128)}, f32[1,512,512]{2,1,0:T(8,128)}, u32[]{:S(2)}, u32[]{:S(2)}) %collective-permute-start.1) | collective-permute-done | bytes 1048608 | tf_op jit(solution)/shard_map/ppermute | solution.py:28
  523.9 7.2 fusion
  531.1 116.0 %all-gather.11.cloned.1.call-done = f32[1,4096,512]{2,1,0:T(8,128)} async-done(((f32[1,512,512]{2,1,0:T(8,128)}), f32[1,4096,512]{2,1,0:T(8,128)}) %all-gather.11.cloned.1.call-update) | async-done | bytes 8388624 | tf_op jit(solution)/shard_map/all_gather | solution.py:103
  651.7 60.7 %subtract_select_fusion.1 = f32[2048,4096]{1,0:T(8,128)} fusion(f32[2048,4096]{1,0:T(8,128)} %fusion, pred[4096]{0:T(1024)(128)(4,1)S(1)} %broadcast_compare_fusion.1, pred[2048]{0:T(1024)(128)(4,1)S(1)} %compare_and_fusion, f32[2048,512]{1,0:T(8,128)S(1)} %copy-done, f32[4096,512]{1,0:T(8,128)S(1)} %bitcast.179), kind=kOutput, calls=%fused_computation.7 | convolution fusion | flops 51564773376 | bytes 79697920 | tf_op jit(solution)/shard_map/dot_general | solution.py:37
  715.6 76.4 %all-reduce.7.cloned.1.call-done = f32[512,512]{0,1:T(8,128)} async-done(((f32[512,512]{0,1:T(8,128)}), f32[512,512]{0,1:T(8,128)}) %all-reduce.7.cloned.1.call-update) | async-done | bytes 1048592 | tf_op jit(solution)/shard_map/psum | solution.py:73
  795.0 11.7 cholesky.446
  806.9 9.8 custom-call.35
  817.4 11.7 cholesky.465
  829.2 10.0 custom-call.36
  839.8 11.7 cholesky.486
  851.6 9.8 custom-call.37
  862.0 11.7 cholesky.503
  880.8 8.1 while.17
  888.9 39.3 %custom-call.38 = f32[4,128,128]{1,2,0:T(8,128)S(1)} custom-call(f32[4,128,128]{2,1,0:T(8,128)S(1)} %get-tuple-element.140), custom_call_target="InvertDiagBlocksLowerTriangular" | custom-call | tf_op jit(solution)/shard_map/jit(_solve_triangular)/triangular_solve | solution.py:76
  933.0 10.5 broadcast_select_fusion
  943.8 105.4 %all-gather.13.cloned.1.call-done = f32[8192,512]{1,0:T(8,128)} async-done(((f32[2048,512]{1,0:T(8,128)}), f32[8192,512]{1,0:T(8,128)}) %all-gather.13.cloned.1.call-update) | async-done | bytes 16777232 | tf_op jit(solution)/shard_map/all_gather | solution.py:11
  1049.2 10.3 reduce_sum.19
  1064.8 91.2 %collective-permute-done.2 = f32[2,512,512]{2,1,0:T(8,128)S(1)} collective-permute-done((f32[2,512,512]{2,1,0:T(8,128)S(1)}, f32[2,512,512]{2,1,0:T(8,128)S(1)}, u32[]{:S(2)}, u32[]{:S(2)}) %collective-permute-start.2) | collective-permute-done | bytes 2097184 | tf_op jit(solution)/shard_map/ppermute | solution.py:28
  1157.3 24.0 %collective-permute-done.3 = f32[1,512,512]{2,1,0:T(8,128)S(1)} collective-permute-done((f32[1,512,512]{2,1,0:T(8,128)S(1)}, f32[1,512,512]{2,1,0:T(8,128)S(1)}, u32[]{:S(2)}, u32[]{:S(2)}) %collective-permute-start.3) | collective-permute-done | bytes 1048608 | tf_op jit(solution)/shard_map/ppermute | solution.py:28
  1190.6 117.4 %all-gather.15.cloned.1.call-done = f32[1,4096,512]{2,1,0:T(8,128)} async-done(((f32[1,512,512]{2,1,0:T(8,128)}), f32[1,4096,512]{2,1,0:T(8,128)}) %all-gather.15.cloned.1.call-update) | async-done | bytes 8388624 | tf_op jit(solution)/shard_map/all_gather | solution.py:103
  1312.5 61.1 %subtract_select_fusion = f32[2048,4096]{1,0:T(8,128)} fusion(f32[2048,4096]{1,0:T(8,128)} %fusion.1, pred[4096]{0:T(1024)(128)(4,1)S(1)} %broadcast_compare_fusion, pred[2048]{0:T(1024)(128)(4,1)S(1)} %compare_and_fusion.1, f32[2048,512]{1,0:T(8,128)S(1)} %copy-done.1, f32[4096,512]{1,0:T(8,128)S(1)} %bitcast.180), kind=kOutput, calls=%fused_computation.6 | convolution fusion | flops 51564773376 | bytes 79697920 | tf_op jit(solution)/shard_map/dot_general | solution.py:37
  1376.6 76.6 %all-reduce.9.cloned.1.call-done = f32[512,512]{0,1:T(8,128)} async-done(((f32[512,512]{0,1:T(8,128)}), f32[512,512]{0,1:T(8,128)}) %all-reduce.9.cloned.1.call-update) | async-done | bytes 1048592 | tf_op jit(solution)/shard_map/psum | solution.py:73
  1456.2 11.7 cholesky.518
  1468.1 9.8 custom-call.39
  1478.6 11.7 cholesky.537
  1490.3 10.0 custom-call.40
  1501.0 11.7 cholesky.558
  1512.7 9.8 custom-call.41
  1523.1 11.9 cholesky.575
  1541.6 8.1 while.18
  1549.7 39.3 %custom-call.42 = f32[4,128,128]{1,2,0:T(8,128)S(1)} custom-call(f32[4,128,128]{2,1,0:T(8,128)S(1)} %get-tuple-element.141), custom_call_target="InvertDiagBlocksLowerTriangular" | custom-call | tf_op jit(solution)/shard_map/jit(_solve_triangular)/triangular_solve | solution.py:76
  1593.9 8.7 fusion.14
  (201 shorter events, 123.7 us)
Async XLA Ops:
  6.5 107.3 %all-reduce.5.cloned.1.call-start = ((), (), s32[]{:S(2)}) async-start(), calls=%async_computation | async-start | bytes 2097152 | tf_op jit(solution)/shard_map/psum | solution.py:73
  32.6 348.3 %all-gather.9.cloned.1.call-start = ((), (), s32[]{:S(2)}) async-start(), calls=%async_computation.3 | async-start | bytes 20971520 | tf_op jit(solution)/shard_map/all_gather | solution.py:11
  113.9 2.8 copy-start.2
  276.2 371.0 %all-gather.11.cloned.1.call-start = ((), (), s32[]{:S(2)}) async-start(), calls=%async_computation.4 | async-start | bytes 9437184 | tf_op jit(solution)/shard_map/all_gather | solution.py:103
  396.0 93.8 %collective-permute-start = (f32[2,512,512]{2,1,0:T(8,128)}, f32[2,512,512]{2,1,0:T(8,128)S(1)}, u32[]{:S(2)}, u32[]{:S(2)}) collective-permute-start(f32[2,512,512]{2,1,0:T(8,128)} %bitcast.14), channel_id=1, source_target_pairs={{0,16},{16,0},{4,20},{20,4},{8,24},{24,8},{12,28},{28,12},{1,17},{... | collective-permute-start | bytes 6291464 | tf_op jit(solution)/shard_map/ppermute | solution.py:28
  489.9 1.3 copy-start.7
  494.4 24.8 %collective-permute-start.1 = (f32[1,512,512]{2,1,0:T(8,128)}, f32[1,512,512]{2,1,0:T(8,128)}, u32[]{:S(2)}, u32[]{:S(2)}) collective-permute-start(f32[1,512,512]{2,1,0:T(8,128)} %slice_select_fusion.5), channel_id=1, source_target_pairs={{0,8},{8,0},{4,12},{12,4},{16,24},{24,16},{20,28},{28,20},{1,9},{9... | collective-permute-start | bytes 3145736 | tf_op jit(solution)/shard_map/ppermute | solution.py:28
  520.6 271.4 %all-reduce.7.cloned.1.call-start = ((), (), s32[]{:S(2)}) async-start(), calls=%async_computation.1 | async-start | bytes 2097152 | tf_op jit(solution)/shard_map/psum | solution.py:73
  647.1 4.6 copy-start
  715.4 333.8 %all-gather.13.cloned.1.call-start = ((), (), s32[]{:S(2)}) async-start(), calls=%async_computation.5 | async-start | bytes 20971520 | tf_op jit(solution)/shard_map/all_gather | solution.py:11
  792.1 1.5 copy-start.3
  943.5 364.4 %all-gather.15.cloned.1.call-start = ((), (), s32[]{:S(2)}) async-start(), calls=%async_computation.6 | async-start | bytes 9437184 | tf_op jit(solution)/shard_map/all_gather | solution.py:103
  1062.3 93.7 %collective-permute-start.2 = (f32[2,512,512]{2,1,0:T(8,128)S(1)}, f32[2,512,512]{2,1,0:T(8,128)S(1)}, u32[]{:S(2)}, u32[]{:S(2)}) collective-permute-start(f32[2,512,512]{2,1,0:T(8,128)S(1)} %bitcast.193), channel_id=1, source_target_pairs={{0,16},{16,0},{4,20},{20,4},{8,24},{24,8},{12,28},{28,12},{1,17},{... | collective-permute-start | bytes 6291464 | tf_op jit(solution)/shard_map/ppermute | solution.py:28
  1156.5 26.3 %copy-start.5 = (f32[512,512]{1,0:T(8,128)S(1)}, f32[512,512]{1,0:T(8,128)}, u32[]{:S(2)}) copy-start(f32[512,512]{1,0:T(8,128)} %get-tuple-element.169) | copy-start | bytes 3145732
  1156.7 24.5 %collective-permute-start.3 = (f32[1,512,512]{2,1,0:T(8,128)S(1)}, f32[1,512,512]{2,1,0:T(8,128)S(1)}, u32[]{:S(2)}, u32[]{:S(2)}) collective-permute-start(f32[1,512,512]{2,1,0:T(8,128)S(1)} %slice_select_fusion.4), channel_id=1, source_target_pairs={{0,8},{8,0},{4,12},{12,4},{16,24},{24,16},{20,28},{28,20},{1,9},{9... | collective-permute-start | bytes 3145736 | tf_op jit(solution)/shard_map/ppermute | solution.py:28
  1182.7 270.6 %all-reduce.9.cloned.1.call-start = ((), (), s32[]{:S(2)}) async-start(), calls=%async_computation.2 | async-start | bytes 2097152 | tf_op jit(solution)/shard_map/psum | solution.py:73
  1307.9 4.6 copy-start.1
  1453.2 1.5 copy-start.4
  1593.8 8.7 copy-start.6
Sparse Core Ops, SparseCore 0:
  32.7 81.0 all-reduce.4
  276.3 104.5 all-gather.8
  520.8 126.3 all-gather.10
  715.5 76.5 all-reduce.6
  943.7 105.4 all-gather.12
  1182.8 125.1 all-gather.14
  1376.7 76.4 all-reduce.8
